TPU v7x, 256 devices: a whole 4x4x8 slice. The times are simulated.
256 devices in a mesh: ctx: 16 (over x, y), tp: 16 (over z, core).
Axes of the slice: x: 4, y: 4, z: 8, core: 2. Of those that a mesh axis runs over, the one named last changes fastest.
Arguments:
- tokens: bfloat16 [16384, 2560], P(('ctx', 'tp')), may hold values from -8 to 8
- norm1_gain: float32 [2560], replicated, may hold values from 0.1 to 1.9
- w_z: bfloat16 [2560, 5120], P(None, 'tp'), may hold values from -0.125 to 0.125
- w_x: bfloat16 [2560, 5120], P(None, 'tp'), may hold values from -0.125 to 0.125
- w_bc: bfloat16 [2560, 256], replicated, may hold values from -0.125 to 0.125
- w_dt: bfloat16 [2560, 80], P(None, 'tp'), may hold values from -1 to 1
- dt_bias: float32 [80], P('tp'), may hold values from -5.5 to -4
- a_log: float32 [80], P('tp'), may hold values from -12 to 1.4
- conv_x: float32 [4, 5120], P(None, 'tp'), may hold values from -3 to 3
- conv_bc: float32 [4, 256], replicated, may hold values from -3 to 3
- d_skip: float32 [80], P('tp'), may hold values from 0.1 to 1.9
- ssm_gain: float32 [5120], P('tp'), may hold values from 0.1 to 1.9
- w_out: bfloat16 [5120, 2560], P('tp'), may hold values from -0.078125 to 0.078125
- norm2_gain: float32 [2560], replicated, may hold values from 0.1 to 1.9
- w_gate: bfloat16 [2560, 5120], P(None, 'tp'), may hold values from -0.125 to 0.125
- w_up: bfloat16 [2560, 5120], P(None, 'tp'), may hold values from -0.125 to 0.125
- w_down: bfloat16 [5120, 2560], P('tp'), may hold values from -0.078125 to 0.078125
Outputs:
- layer_out: bfloat16 [16384, 2560], P(('ctx', 'tp'))
All inputs are finite; a program needn't handle non-finite values.
Results may differ from a plain program's by a relative error of at most 0.017.
Values may be sent and summed in bfloat16 or wider, within the bound.
No kernel may reach another device: no remote copies, remote signals or barrier semaphores. Data moves between devices by JAX's collectives and lax.ppermute only.
A program may use at most 128 MiB of HBM per device.

v0:
```python
import jax
import jax.numpy as jnp
from jax import lax
from jax.sharding import PartitionSpec as P

HEADS = 80
HEAD_DIM = 64
STATE_DIM = 128
BLOCK_LEN = 256
EPS = 1e-05


def from_behind(value, axis, steps):
    count = lax.axis_size(axis)
    first, last = (max(0, -steps), min(count, count - steps))
    return lax.ppermute(value, axis, [(source, source + steps) for source in range(first, last)])


def carried_in(shard, axis, join, neutral):
    place = lax.axis_index(axis)
    gathered = jax.tree.map(
        lambda a, kind: lax.all_gather(a.astype(kind), axis), shard, (jnp.bfloat16, jnp.bfloat16)
    )
    state = jax.tree.map(lambda a, e: jnp.zeros_like(a) + jnp.asarray(e, a.dtype), shard, neutral)

    def one(step, state):
        return join(
            state,
            jax.tree.map(
                lambda a, own: lax.dynamic_index_in_dim(a, step, 0, False).astype(own.dtype),
                gathered,
                shard,
            ),
        )

    return lax.fori_loop(0, place, one, state)


def rms_rows(values, gain):
    wide = values.astype(jnp.float32)
    return wide * lax.rsqrt(jnp.mean(wide * wide, axis=-1, keepdims=True) + EPS) * gain


def conv_four(rim, current, kernel):
    extended = jnp.concatenate([rim, current], axis=0).astype(jnp.float32)
    length = current.shape[0]
    result = kernel[0] * extended[0:length]
    for offset in range(1, 4):
        result = result + kernel[offset] * extended[offset : offset + length]
    return result


def combine_states(prior_part, next_part):
    return (
        prior_part[0] * next_part[0],
        next_part[1] + next_part[0][:, None, None] * prior_part[1],
    )


def carry_step(state, pieces):
    decay_now, fresh = pieces
    return (decay_now[:, None, None] * state + fresh, state)


def local(
    tokens,
    norm1_gain,
    w_z,
    w_x,
    w_bc,
    w_dt,
    dt_bias,
    a_log,
    conv_x,
    conv_bc,
    d_skip,
    ssm_gain,
    w_out,
    norm2_gain,
    w_gate,
    w_up,
    w_down,
):
    gathered = lax.all_gather(tokens, "tp", axis=0, tiled=True)
    normed = rms_rows(gathered, norm1_gain).astype(jnp.bfloat16)
    bc_rows = jnp.dot(normed, w_bc, preferred_element_type=jnp.float32).astype(jnp.bfloat16)
    group_len = gathered.shape[0]
    head_count = w_dt.shape[1]
    channels = w_x.shape[1]
    gate_z = jnp.dot(normed, w_z, preferred_element_type=jnp.float32)
    inner_rows = jnp.dot(normed, w_x, preferred_element_type=jnp.float32).astype(jnp.bfloat16)
    dt_raw = jnp.dot(normed, w_dt, preferred_element_type=jnp.float32)
    rim_inner, rim_bc = from_behind((inner_rows[-3:], bc_rows[-3:]), "ctx", 1)
    conv_inner = jax.nn.silu(conv_four(rim_inner, inner_rows, conv_x)).astype(jnp.bfloat16)
    conv_bcm = jax.nn.silu(conv_four(rim_bc, bc_rows, conv_bc)).astype(jnp.bfloat16)
    dt_step = jax.nn.softplus(dt_raw + dt_bias)
    log_decay = -dt_step * jnp.exp(a_log)
    block_count = group_len // BLOCK_LEN
    log_blocks = log_decay.reshape(block_count, BLOCK_LEN, head_count)
    step_blocks = dt_step.reshape(block_count, BLOCK_LEN, head_count)
    cum_decay = jnp.cumsum(log_blocks, axis=1)
    b_mat = conv_bcm[:, :STATE_DIM].reshape(block_count, BLOCK_LEN, STATE_DIM)
    c_mat = conv_bcm[:, STATE_DIM:].reshape(block_count, BLOCK_LEN, STATE_DIM)
    scores = jnp.einsum("btn,bsn->bts", c_mat, b_mat, preferred_element_type=jnp.float32)
    causal_mask = jnp.tril(jnp.ones((BLOCK_LEN, BLOCK_LEN), dtype=bool))[None, :, :, None]
    decay_diff = jnp.where(causal_mask, cum_decay[:, :, None, :] - cum_decay[:, None, :, :], 0.0)
    weights = jnp.where(causal_mask, jnp.exp(decay_diff), 0.0)
    inner_wide = conv_inner.astype(jnp.float32).reshape(
        block_count, BLOCK_LEN, head_count, HEAD_DIM
    )
    scaled = inner_wide * step_blocks[..., None]
    mixed_w = scores[..., None] * weights
    y_intra = jnp.einsum("btsh,bshp->bthp", mixed_w, scaled, precision=lax.Precision.HIGHEST)
    block_last = cum_decay[:, -1, :]
    tail_decay = jnp.exp(block_last[:, None, :] - cum_decay)
    b_wide = b_mat.astype(jnp.float32)
    c_wide = c_mat.astype(jnp.float32)
    block_states = jnp.einsum(
        "bsh,bshp,bsn->bhpn", tail_decay, scaled, b_wide, precision=lax.Precision.HIGHEST
    )
    block_decay = jnp.exp(block_last)
    zero_state = jnp.zeros((head_count, HEAD_DIM, STATE_DIM), jnp.float32)
    local_final, local_in = lax.scan(carry_step, zero_state, (block_decay, block_states))
    total_decay = jnp.prod(block_decay, axis=0)
    prior_decay = jnp.exp(jnp.cumsum(block_last, axis=0) - block_last)
    identity = (jnp.ones((head_count,), jnp.float32), zero_state)
    incoming_decay, incoming = carried_in(
        (total_decay, local_final), "ctx", combine_states, identity
    )
    state_in = local_in + prior_decay[:, :, None, None] * incoming[None]
    y_inter = jnp.exp(cum_decay)[..., None] * jnp.einsum(
        "btn,bhpn->bthp", c_wide, state_in, precision=lax.Precision.HIGHEST
    )
    ssm_out = y_intra + y_inter + d_skip[None, None, :, None] * inner_wide
    gated = ssm_out.reshape(group_len, channels) * jax.nn.silu(gate_z)
    squares = lax.psum(jnp.sum(gated * gated, axis=-1), "tp")
    scaled_out = (gated * lax.rsqrt(squares / (HEADS * HEAD_DIM) + EPS)[:, None] * ssm_gain).astype(
        jnp.bfloat16
    )
    piece = scaled_out
    mixer_own = lax.psum_scatter(
        jnp.dot(piece, w_out, preferred_element_type=jnp.float32).astype(jnp.bfloat16),
        "tp",
        scatter_dimension=0,
        tiled=True,
    ).astype(jnp.float32)
    resid = (tokens.astype(jnp.float32) + mixer_own).astype(jnp.bfloat16)
    normed_own = rms_rows(resid, norm2_gain).astype(jnp.bfloat16)
    mlp_in = lax.all_gather(normed_own, "tp", axis=0, tiled=True)
    mlp_gate = jnp.dot(mlp_in, w_gate, preferred_element_type=jnp.float32)
    mlp_up = jnp.dot(mlp_in, w_up, preferred_element_type=jnp.float32)
    hidden = (jax.nn.silu(mlp_gate) * mlp_up).astype(jnp.bfloat16)
    piece = hidden
    mlp_down = lax.psum_scatter(
        jnp.dot(piece, w_down, preferred_element_type=jnp.float32).astype(jnp.bfloat16),
        "tp",
        scatter_dimension=0,
        tiled=True,
    ).astype(jnp.float32)
    return (resid.astype(jnp.float32) + mlp_down).astype(jnp.bfloat16)


def solution(mesh):
    return jax.shard_map(
        local,
        mesh=mesh,
        in_specs=(
            P(("ctx", "tp"), None),
            P(),
            P(None, "tp"),
            P(None, "tp"),
            P(),
            P(None, "tp"),
            P("tp"),
            P("tp"),
            P(None, "tp"),
            P(),
            P("tp"),
            P("tp"),
            P("tp", None),
            P(),
            P(None, "tp"),
            P(None, "tp"),
            P("tp", None),
        ),
        out_specs=P(("ctx", "tp"), None),
        check_vma=False,
    )
```

profile of v0, /device:TPU:4, one launch (start us, length us, event | category | flops | bytes accessed | tf_op | source)
XLA Modules:
  0.0 396.0 jit_solution(1112012405852655867)
XLA Ops:
  9.7 45.6 %all-gather.6.cloned.1.call-done = bf16[1024,2560]{1,0:T(8,128)(2,1)} async-done(((bf16[64,2560]{1,0:T(8,128)(2,1)}), bf16[1024,2560]{1,0:T(8,128)(2,1)}) %all-gather.6.cloned.1.call-update) | async-done | bytes 5242896 | tf_op jit(solution)/shard_map/all_gather | solution.py:84
  55.3 3.7 fusion.1
  63.0 6.0 %reduce-window.6 = f32[4,5,2,128]{3,2,1,0:T(2,128)S(1)} reduce-window(f32[4,5,2,128]{3,2,1,0:T(2,128)S(1)} %copy.46, f32[]{:T(128)} %constant.61.clone.1), window={size=1x1x1x128 pad=0_0x0_0x0_0x127_0}, to_apply=%region_1.2 | reduce-window | flops 650240 | bytes 40964 | tf_op jit(solution)/shard_map/reduce-window
  70.0 4.5 %convolution_convert_fusion.3 = bf16[1024,256]{1,0:T(8,128)(2,1)S(1)} fusion(bf16[1024,2560]{1,0:T(8,128)(2,1)} %copy-done.1, bf16[2560,256]{1,0:T(8,128)(2,1)} %param.25), kind=kOutput, calls=%fused_computation.44 | convolution fusion | flops 1342439424 | bytes 7077888 | tf_op jit(solution)/shard_map/dot_general | solution.py:86
  74.5 3.4 collective-permute-start.1
  80.0 3.4 collective-permute-start
  84.2 4.2 %collective-permute-done = bf16[3,320]{0,1:T(8,128)(2,1)S(1)} collective-permute-done((bf16[3,320]{0,1:T(8,128)(2,1)S(1)}, bf16[3,320]{0,1:T(8,128)(2,1)S(1)}, u32[]{:S(2)}, u32[]{:S(2)}) %collective-permute-start) | collective-permute-done | bytes 1952 | tf_op jit(solution)/shard_map/ppermute | solution.py:16
  88.7 2.4 fusion.40
  91.2 2.8 reshape.107
  94.0 2.2 fusion.24
  96.2 3.2 while.26
  101.7 31.3 %all-reduce = bf16[80]{0:T(256)(128)(2,1)S(1)} all-reduce(bf16[80]{0:T(256)(128)(2,1)S(1)} %dynamic-update-slice), channel_id=3, replica_groups=mesh['ctx'=16,'tp'=16] {'ctx'}, use_global_device_ids=true, to_apply=%add | all-reduce | flops 80 | bytes 320
  133.4 8.5 %fusion.17 = f32[4,256,5,64]{1,3,2,0:T(8,128)} fusion(f32[4,256,5]{1,2,0:T(8,128)S(1)} %copy.50, f32[4,256,256]{2,1,0:T(8,128)S(1)} %fusion.50, pred[256,256]{1,0:T(8,128)(4,1)S(1)} %iota_compare_fusion, f32[4,256,5,64]{1,0,3,2:T(4,128)} %reshape.107, f32[4,256,5]{1,2,0:T(8,128)S(1)} %bitcast.98), kind=kOutput, calls=%fused_computation.28 | convolution fusion | flops 1012203520 | bytes 3776512 | tf_op jit(solution)/shard_map/btsh,bshp->bthp/dot_general | solution.py:113
  141.9 2.0 all-gather.10.cloned.1.call-done
  143.9 8.3 %while.25 = (s32[]{:T(128)}, f32[5,64,128]{2,1,0:T(8,128)S(1)}, s32[]{:T(128)}, bf16[16,5,64,128]{3,2,1,0:T(8,128)(2,1)}, bf16[16,5]{1,0:T(8,128)(2,1)S(1)}, /*index=5*/s32[]{:T(128)}, s32[]{:T(128)}, s32[]{:T(128)}) while((s32[]{:T(128)}, f32[5,64,128]{2,1,0:T(8,128)S(1)}, s32[]{:T(128)}, bf16[16,5,64,128]{3,2,1,0:T(8,128)(2,1)}, ...), condition=%wide.region_8.9_spmd, body=%wide.region_7.8_spmd.sunk | while | flops 122890 | bytes 409785 | solution.py:36
  152.2 3.0 fusion.16
  158.0 3.1 multiply_reduce_fusion
  161.1 23.9 %psum.7 = f32[1024]{0:T(1024)S(1)} all-reduce(f32[1024]{0:T(1024)S(1)} %get-tuple-element.135), channel_id=1, replica_groups=mesh['ctx'=16,'tp'=16] {'tp'}, use_global_device_ids=true, to_apply=%region_10.11 | all-reduce | flops 1024 | bytes 8192 | tf_op jit(solution)/shard_map/psum | solution.py:136
  185.1 6.8 %convolution_convert_fusion.1 = bf16[1024,2560]{1,0:T(8,128)(2,1)} fusion(bf16[320,2560]{1,0:T(8,128)(2,1)S(1)} %copy-done, f32[320]{0:T(512)S(1)} %copy-done.13, f32[1024]{0:T(1024)S(1)} %add_rsqrt_fusion, f32[1024,320]{0,1:T(8,128)} %bitcast.94, f32[1024,320]{0,1:T(8,128)} %get-tuple-element.136), kind=kOutput, calls=%fused_computation.12 | convolution fusion | flops 1682964480 | bytes 9508096 | tf_op jit(solution)/shard_map/dot_general | solution.py:142
  192.0 71.4 %reduce-scatter.3.cloned.1.call-done = bf16[64,2560]{1,0:T(8,128)(2,1)} async-done(((bf16[1024,2560]{1,0:T(8,128)(2,1)}), bf16[64,2560]{1,0:T(8,128)(2,1)}) %reduce-scatter.3.cloned.1.call-update) | async-done | bytes 327696 | tf_op jit(solution)/shard_map/reduce_scatter | solution.py:141
  266.7 41.6 %all-gather.8.cloned.1.call-done = bf16[1024,2560]{1,0:T(8,128)(2,1)} async-done(((bf16[64,2560]{1,0:T(8,128)(2,1)}), bf16[1024,2560]{1,0:T(8,128)(2,1)}) %all-gather.8.cloned.1.call-update) | async-done | bytes 5242896 | tf_op jit(solution)/shard_map/all_gather | solution.py:149
  308.3 4.9 %fusion.51 = f32[1024,320]{0,1:T(8,128)S(1)} fusion(bf16[1024,2560]{1,0:T(8,128)(2,1)} %all-gather.8.cloned.1.call-done, bf16[2560,320]{0,1:T(8,128)(2,1)} %param.35), kind=kOutput, calls=%fused_computation.98 | convolution fusion | flops 1677721600 | bytes 8192000 | tf_op jit(solution)/shard_map/dot_general | solution.py:150
  313.2 10.4 %convolution_convert_fusion = bf16[1024,2560]{1,0:T(8,128)(2,1)} fusion(bf16[320,2560]{1,0:T(8,128)(2,1)} %param.37, bf16[1024,2560]{1,0:T(8,128)(2,1)} %all-gather.8.cloned.1.call-done, bf16[2560,320]{0,1:T(8,128)(2,1)} %param.36, f32[1024,320]{0,1:T(8,128)S(1)} %fusion.51), kind=kOutput, calls=%fused_computation.11 | convolution fusion | flops 3360030720 | bytes 15073280 | tf_op jit(solution)/shard_map/dot_general | solution.py:155
  323.6 64.0 %reduce-scatter.5.cloned.1.call-done = bf16[64,2560]{1,0:T(8,128)(2,1)} async-done(((bf16[1024,2560]{1,0:T(8,128)(2,1)}), bf16[64,2560]{1,0:T(8,128)(2,1)}) %reduce-scatter.5.cloned.1.call-update) | async-done | bytes 327696 | tf_op jit(solution)/shard_map/reduce_scatter | solution.py:154
  (129 shorter events, 32.1 us)
Async XLA Ops:
  6.5 178.5 %copy-start = (bf16[320,2560]{1,0:T(8,128)(2,1)S(1)}, bf16[320,2560]{1,0:T(8,128)(2,1)}, u32[]{:S(2)}) copy-start(bf16[320,2560]{1,0:T(8,128)(2,1)} %param.33) | copy-start | bytes 4915204
  6.5 48.8 %all-gather.6.cloned.1.call-start = ((), (), s32[]{:S(2)}) async-start(), calls=%async_computation.2 | async-start | bytes 5570560 | tf_op jit(solution)/shard_map/all_gather | solution.py:84
  7.3 136.6 %all-gather.10.cloned.1.call-start = ((), (), s32[]{:S(2)}) async-start(), calls=%async_computation.6 | async-start | bytes 1392640 | tf_op jit(solution)/shard_map/all_gather | solution.py:22
  9.7 49.3 %copy-start.7 = (f32[2560]{0:T(1024)S(1)}, f32[2560]{0:T(1024)}, u32[]{:S(2)}) copy-start(f32[2560]{0:T(1024)} %param.22) | copy-start | bytes 30724
  55.3 4.0 %copy-start.2 = (bf16[1024,2560]{1,0:T(8,128)(2,1)S(1)}, bf16[1024,2560]{1,0:T(8,128)(2,1)}, u32[]{:S(2)}) copy-start(bf16[1024,2560]{1,0:T(8,128)(2,1)} %all-gather.6.cloned.1.call-done) | copy-start | bytes 15728644
  60.6 2.3 copy-start.1
  69.5 8.4 %slice-start = ((s8[5242880]{0:T(1024)(128)(4,1)}), s8[1048576]{0:T(1024)(128)(4,1)S(1)}, s32[]{:S(2)}) async-start(s8[5242880]{0:T(1024)(128)(4,1)} %bitcast.84), calls=%async_computation.7 | async-start | bytes 2097152
  70.0 8.0 %slice-start.1 = ((s8[5242880]{0:T(1024)(128)(4,1)}), s8[4194304]{0:T(1024)(128)(4,1)S(1)}, s32[]{:S(2)}) async-start(s8[5242880]{0:T(1024)(128)(4,1)} %bitcast.84), calls=%async_computation.8 | async-start | bytes 8388608
  70.0 8.0 %copy-start.11 = (bf16[2560,320]{0,1:T(8,128)(2,1)S(1)}, bf16[2560,320]{0,1:T(8,128)(2,1)}, u32[]{:S(2)}) copy-start(bf16[2560,320]{0,1:T(8,128)(2,1)} %param.24) | copy-start | bytes 4915204
  74.5 8.9 %collective-permute-start.1 = (bf16[3,256]{1,0:T(4,128)(2,1)S(1)}, bf16[3,256]{1,0:T(4,128)(2,1)S(1)}, u32[]{:S(2)}, u32[]{:S(2)}) collective-permute-start(bf16[3,256]{1,0:T(4,128)(2,1)S(1)} %slice.97), channel_id=1, source_target_pairs={{0,16},{16,32},{32,48},{48,64},{64,80},{80,96},{96,112},{112,128},... | collective-permute-start | bytes 4616 | tf_op jit(solution)/shard_map/ppermute | solution.py:16
  80.0 8.4 %collective-permute-start = (bf16[3,320]{0,1:T(8,128)(2,1)S(1)}, bf16[3,320]{0,1:T(8,128)(2,1)S(1)}, u32[]{:S(2)}, u32[]{:S(2)}) collective-permute-start(bf16[3,320]{0,1:T(8,128)(2,1)S(1)} %slice.92), channel_id=1, source_target_pairs={{0,16},{16,32},{32,48},{48,64},{64,80},{80,96},{96,112},{112,128},... | collective-permute-start | bytes 5768 | tf_op jit(solution)/shard_map/ppermute | solution.py:16
  96.1 4.0 %copy-start.14 = (u32[256]{0:T(256)S(1)}, u32[256]{0:T(256)}, u32[]{:S(2)}) copy-start(u32[256]{0:T(256)} %constant.76) | copy-start | bytes 3076
  100.0 163.3 %reduce-scatter.3.cloned.1.call-start = ((), (), s32[]{:S(2)}) async-start(), calls=%async_computation.3 | async-start | bytes 5570560 | tf_op jit(solution)/shard_map/reduce_scatter | solution.py:141
  141.9 10.3 %copy-start.10 = (f32[5]{0:T(128)S(1)}, f32[5]{0:T(128)}, u32[]{:S(2)}) copy-start(f32[5]{0:T(128)} %param.31) | copy-start | bytes 64
  143.9 12.5 %slice-start.2 = ((s8[5242880]{0:T(1024)(128)(4,1)}), s8[1048576]{0:T(1024)(128)(4,1)S(1)}, s32[]{:S(2)}) async-start(s8[5242880]{0:T(1024)(128)(4,1)} %bitcast.86), calls=%async_computation.9 | async-start | bytes 2097152
  152.2 4.2 %slice-start.3 = ((s8[5242880]{0:T(1024)(128)(4,1)}), s8[4194304]{0:T(1024)(128)(4,1)S(1)}, s32[]{:S(2)}) async-start(s8[5242880]{0:T(1024)(128)(4,1)} %bitcast.86), calls=%async_computation.10 | async-start | bytes 8388608
  156.1 1.9 copy-start.12
  156.4 4.7 %copy-start.5 = (f32[40,8,4,256]{3,1,2,0:T(8,128)}, f32[40,8,4,256]{3,1,2,0:T(8,128)S(1)}, u32[]{:S(2)}) copy-start(f32[40,8,4,256]{3,1,2,0:T(8,128)S(1)} %copy.60) | copy-start | bytes 3932164
  158.0 27.1 %copy-start.13 = (f32[320]{0:T(512)S(1)}, f32[320]{0:T(512)}, u32[]{:S(2)}) copy-start(f32[320]{0:T(512)} %param.32) | copy-start | bytes 3844
  191.9 71.5 %copy-start.3 = (bf16[64,2560]{1,0:T(8,128)(2,1)S(1)}, bf16[64,2560]{1,0:T(8,128)(2,1)}, u32[]{:S(2)}) copy-start(bf16[64,2560]{1,0:T(8,128)(2,1)} %param.21) | copy-start | bytes 983044
  191.9 72.7 %copy-start.8 = (f32[2560]{0:T(1024)S(1)}, f32[2560]{0:T(1024)}, u32[]{:S(2)}) copy-start(f32[2560]{0:T(1024)} %param.34) | copy-start | bytes 30724
  191.9 116.4 %all-gather.8.cloned.1.call-start = ((), (), s32[]{:S(2)}) async-start(), calls=%async_computation.4 | async-start | bytes 5570560 | tf_op jit(solution)/shard_map/all_gather | solution.py:149
  266.4 121.2 %reduce-scatter.5.cloned.1.call-start = ((), (), s32[]{:S(2)}) async-start(), calls=%async_computation.5 | async-start | bytes 5570560 | tf_op jit(solution)/shard_map/reduce_scatter | solution.py:154
  323.6 64.0 %copy-start.4 = (bf16[64,2560]{1,0:T(8,128)(2,1)S(1)}, bf16[64,2560]{1,0:T(8,128)(2,1)}, u32[]{:S(2)}) copy-start(bf16[64,2560]{1,0:T(8,128)(2,1)} %reduce-scatter.3.cloned.1.call-done) | copy-start | bytes 983044
  (2 other events, 2.6 us)
Sparse Core Ops, SparseCore 0:
  9.2 46.0 all-gather.5
  100.2 43.6 all-gather.9
  192.1 71.2 reduce-scatter.2
  266.5 41.7 all-gather.7
  323.7 63.8 reduce-scatter.4
where the time goes:
time: 397 us; the launch traced here: 396 us
  waiting for transfers between devices  230 us (58%)
  blocking collectives  55.3 us (14%)
  matrix products  47.1 us (12%)
  other arithmetic  31.4 us (8%)
  between operations  14.2 us (4%)
  local copies, waits for them, and re-layouts  10.9 us (3%)
  starting transfers between devices  7.17 us (2%)
    reduce_scatter x1, waiting for transfers between devices, local(): lax.psum_scatter(jnp.dot(piece, w_out, preferred_element_type=jnp.float32...  71.4 us
    reduce_scatter x1, waiting for transfers between devices, local(): lax.psum_scatter(jnp.dot(piece, w_down, preferred_element_type=jnp.float3...  64 us
    all_gather x1, waiting for transfers between devices, local(): gathered = lax.all_gather(tokens, 'tp', axis=0, tiled=True)  45.6 us
    all_gather x1, waiting for transfers between devices, local(): mlp_in = lax.all_gather(normed_own, 'tp', axis=0, tiled=True)  41.6 us
    unnamed x1, blocking collectives  31.3 us
    psum x1, blocking collectives, local(): squares = lax.psum(jnp.sum(gated * gated, axis=-1), 'tp')  23.9 us
    dot_general x1, matrix products, local(): jnp.dot(piece, w_down, preferred_element_type=jnp.float32)  10.4 us
    dot_general x1, matrix products, local(): jnp.einsum('btsh,bshp->bthp', mixed_w, scaled, precision=lax.Precision.HI...  8.52 us
  transfers between devices with their start and end apart: 7, of which 6 were waited for; matrix products, arithmetic and copies ran while one was open for 4% of the time, Pallas kernels for 0%

commit v1 on v0

--- a/solution.py
+++ b/solution.py
@@ -8,6 +8,11 @@
 STATE_DIM = 128
 BLOCK_LEN = 256
 EPS = 1e-05
+
+
+def exchange_gather(block, axis, dim):
+    outgoing = jnp.stack([block] * lax.axis_size(axis))
+    return jnp.concatenate(lax.all_to_all(outgoing, axis, 0, 0), axis=dim)
 
 
 def from_behind(value, axis, steps):
@@ -81,7 +86,7 @@
     w_up,
     w_down,
 ):
-    gathered = lax.all_gather(tokens, "tp", axis=0, tiled=True)
+    gathered = exchange_gather(tokens, "tp", 0)
     normed = rms_rows(gathered, norm1_gain).astype(jnp.bfloat16)
     bc_rows = jnp.dot(normed, w_bc, preferred_element_type=jnp.float32).astype(jnp.bfloat16)
     group_len = gathered.shape[0]

time: 397 us -> 481 us (1.21)
  waiting for transfers between devices: 230 us -> 300 us
  starting transfers between devices: 7.17 us -> 16.1 us
    all_to_all x0 -> x1, waiting for transfers between devices: none -> 117 us  [exchange_gather(): return jnp.concatenate(lax.all_to_all(outgoing, axis, 0, 0), axis=dim)]
    all_gather x1 -> x0, waiting for transfers between devices: 45.6 us -> none  [local(): gathered = lax.all_gather(tokens, 'tp', axis=0, tiled=True)]
    all_to_all x0 -> x1, starting transfers between devices: none -> 8.75 us  [exchange_gather(): return jnp.concatenate(lax.all_to_all(outgoing, axis, 0, 0), axis=dim)]
  transfers between devices with their start and end apart: 7 -> 7, of which waited for: 6 -> 6; matrix products, arithmetic and copies ran while one was open for 4% -> 3% of each run, Pallas kernels for 0% -> 0%
where the time goes in v1:
time: 481 us; the launch traced here: 479 us
  waiting for transfers between devices  300 us (62%)
  blocking collectives  55.2 us (11%)
  matrix products  47.1 us (10%)
  other arithmetic  33.7 us (7%)
  starting transfers between devices  16.1 us (3%)
  between operations  14.3 us (3%)
  local copies, waits for them, and re-layouts  12.3 us (3%)
    all_to_all x1, waiting for transfers between devices, exchange_gather(): return jnp.concatenate(lax.all_to_all(outgoing, axis, 0, 0), axis=dim)  117 us
    reduce_scatter x1, waiting for transfers between devices, local(): lax.psum_scatter(jnp.dot(piece, w_out, preferred_element_type=jnp.float32...  71.4 us
    reduce_scatter x1, waiting for transfers between devices, local(): lax.psum_scatter(jnp.dot(piece, w_down, preferred_element_type=jnp.float3...  64 us
    all_gather x1, waiting for transfers between devices, local(): mlp_in = lax.all_gather(normed_own, 'tp', axis=0, tiled=True)  41.6 us
    unnamed x1, blocking collectives  31.3 us
    psum x1, blocking collectives, local(): squares = lax.psum(jnp.sum(gated * gated, axis=-1), 'tp')  24 us
    dot_general x1, matrix products, local(): jnp.dot(piece, w_down, preferred_element_type=jnp.float32)  10.4 us
  transfers between devices with their start and end apart: 7, of which 6 were waited for; matrix products, arithmetic and copies ran while one was open for 3% of the time, Pallas kernels for 0%

profile of v1, /device:TPU:4, one launch (start us, length us, event | category | flops | bytes accessed | tf_op | source)
XLA Modules:
  0.0 479.3 jit_solution(4969441931090197968)
XLA Ops:
  6.5 3.9 stack.2
  10.5 8.7 %all-to-all-start = ((bf16[16,64,2560]{2,1,0:T(8,128)(2,1)}), bf16[16,64,2560]{2,1,0:T(8,128)(2,1)}, u32[]{:S(2)}, u32[]{:S(2)}) async-start(bf16[16,64,2560]{2,1,0:T(8,128)(2,1)} %stack.2), calls=%async_computation | async-start | bytes 10485760 | tf_op jit(solution)/shard_map/all_to_all | solution.py:15
  19.4 116.6 %all-to-all-done = bf16[16,64,2560]{2,1,0:T(8,128)(2,1)} async-done(((bf16[16,64,2560]{2,1,0:T(8,128)(2,1)}), bf16[16,64,2560]{2,1,0:T(8,128)(2,1)}, u32[]{:S(2)}, u32[]{:S(2)}) %all-to-all-start) | async-done | bytes 5242912 | tf_op jit(solution)/shard_map/all_to_all | solution.py:15
  136.0 3.6 multiply_reduce_fusion
  139.7 3.8 fusion.2
  145.8 6.0 %reduce-window.6 = f32[4,5,2,128]{3,2,1,0:T(2,128)S(1)} reduce-window(f32[4,5,2,128]{3,2,1,0:T(2,128)S(1)} %copy.60, f32[]{:T(128)} %constant.61.clone.1), window={size=1x1x1x128 pad=0_0x0_0x0_0x127_0}, to_apply=%region_1.2 | reduce-window | flops 650240 | bytes 40964 | tf_op jit(solution)/shard_map/reduce-window
  152.8 4.5 convolution_convert_fusion.3
  157.4 3.5 collective-permute-start.1
  162.9 3.5 collective-permute-start
  167.3 4.1 collective-permute-done
  174.1 2.8 reshape.122
  179.1 3.2 while.26
  184.7 31.3 %all-reduce = bf16[80]{0:T(256)(128)(2,1)S(1)} all-reduce(bf16[80]{0:T(256)(128)(2,1)S(1)} %dynamic-update-slice), channel_id=3, replica_groups=mesh['ctx'=16,'tp'=16] {'ctx'}, use_global_device_ids=true, to_apply=%add | all-reduce | flops 80 | bytes 320
  216.3 8.5 %fusion.16 = f32[4,256,5,64]{1,3,2,0:T(8,128)} fusion(f32[4,256,5]{1,2,0:T(8,128)S(1)} %copy.64, f32[4,256,256]{2,1,0:T(8,128)S(1)} %fusion.49, pred[256,256]{1,0:T(8,128)(4,1)S(1)} %iota_compare_fusion, f32[4,256,5,64]{1,0,3,2:T(4,128)} %reshape.122, f32[4,256,5]{1,2,0:T(8,128)S(1)} %bitcast.104), kind=kOutput, calls=%fused_computation.27 | convolution fusion | flops 1012203520 | bytes 3776512 | tf_op jit(solution)/shard_map/btsh,bshp->bthp/dot_general | solution.py:118
  227.3 8.3 %while.25 = (s32[]{:T(128)}, f32[5,64,128]{2,1,0:T(8,128)S(1)}, s32[]{:T(128)}, bf16[16,5,64,128]{3,2,1,0:T(8,128)(2,1)}, bf16[16,5]{1,0:T(8,128)(2,1)S(1)}, /*index=5*/s32[]{:T(128)}, s32[]{:T(128)}, s32[]{:T(128)}) while((s32[]{:T(128)}, f32[5,64,128]{2,1,0:T(8,128)S(1)}, s32[]{:T(128)}, bf16[16,5,64,128]{3,2,1,0:T(8,128)(2,1)}, ...), condition=%wide.region_8.9_spmd, body=%wide.region_7.8_spmd.sunk | while | flops 122890 | bytes 409785 | solution.py:41
  235.6 3.0 fusion.15
  241.4 3.1 multiply_reduce_fusion.1
  244.5 24.0 %psum.7 = f32[1024]{0:T(1024)S(1)} all-reduce(f32[1024]{0:T(1024)S(1)} %get-tuple-element.135), channel_id=1, replica_groups=mesh['ctx'=16,'tp'=16] {'tp'}, use_global_device_ids=true, to_apply=%region_10.11 | all-reduce | flops 1024 | bytes 8192 | tf_op jit(solution)/shard_map/psum | solution.py:141
  268.5 6.8 %convolution_convert_fusion.1 = bf16[1024,2560]{1,0:T(8,128)(2,1)} fusion(bf16[320,2560]{1,0:T(8,128)(2,1)S(1)} %copy-done, f32[320]{0:T(512)S(1)} %copy-done.14, f32[1024]{0:T(1024)S(1)} %add_rsqrt_fusion.1, f32[1024,320]{0,1:T(8,128)} %bitcast.100, f32[1024,320]{0,1:T(8,128)} %get-tuple-element.136), kind=kOutput, calls=%fused_computation.11 | convolution fusion | flops 1682964480 | bytes 9508096 | tf_op jit(solution)/shard_map/dot_general | solution.py:147
  275.4 71.4 %reduce-scatter.3.cloned.1.call-done = bf16[64,2560]{1,0:T(8,128)(2,1)} async-done(((bf16[1024,2560]{1,0:T(8,128)(2,1)}), bf16[64,2560]{1,0:T(8,128)(2,1)}) %reduce-scatter.3.cloned.1.call-update) | async-done | bytes 327696 | tf_op jit(solution)/shard_map/reduce_scatter | solution.py:146
  350.1 41.6 %all-gather.5.cloned.1.call-done = bf16[1024,2560]{1,0:T(8,128)(2,1)} async-done(((bf16[64,2560]{1,0:T(8,128)(2,1)}), bf16[1024,2560]{1,0:T(8,128)(2,1)}) %all-gather.5.cloned.1.call-update) | async-done | bytes 5242896 | tf_op jit(solution)/shard_map/all_gather | solution.py:154
  391.7 4.9 %fusion.50 = f32[1024,320]{0,1:T(8,128)S(1)} fusion(bf16[1024,2560]{1,0:T(8,128)(2,1)} %all-gather.5.cloned.1.call-done, bf16[2560,320]{0,1:T(8,128)(2,1)} %param.35), kind=kOutput, calls=%fused_computation.97 | convolution fusion | flops 1677721600 | bytes 8192000 | tf_op jit(solution)/shard_map/dot_general | solution.py:155
  396.6 10.4 %convolution_convert_fusion = bf16[1024,2560]{1,0:T(8,128)(2,1)} fusion(bf16[320,2560]{1,0:T(8,128)(2,1)} %param.37, bf16[1024,2560]{1,0:T(8,128)(2,1)} %all-gather.5.cloned.1.call-done, bf16[2560,320]{0,1:T(8,128)(2,1)} %param.36, f32[1024,320]{0,1:T(8,128)S(1)} %fusion.50), kind=kOutput, calls=%fused_computation.10 | convolution fusion | flops 3360030720 | bytes 15073280 | tf_op jit(solution)/shard_map/dot_general | solution.py:160
  407.0 64.0 %reduce-scatter.5.cloned.1.call-done = bf16[64,2560]{1,0:T(8,128)(2,1)} async-done(((bf16[1024,2560]{1,0:T(8,128)(2,1)}), bf16[64,2560]{1,0:T(8,128)(2,1)}) %reduce-scatter.5.cloned.1.call-update) | async-done | bytes 327696 | tf_op jit(solution)/shard_map/reduce_scatter | solution.py:159
  (134 shorter events, 34.6 us)
Async XLA Ops:
  6.5 262.0 %copy-start = (bf16[320,2560]{1,0:T(8,128)(2,1)S(1)}, bf16[320,2560]{1,0:T(8,128)(2,1)}, u32[]{:S(2)}) copy-start(bf16[320,2560]{1,0:T(8,128)(2,1)} %param.33) | copy-start | bytes 4915204
  10.5 8.8 %copy-start.15 = (f32[5]{0:T(128)S(1)}, f32[5]{0:T(128)}, u32[]{:S(2)}) copy-start(f32[5]{0:T(128)} %param.28) | copy-start | bytes 64
  10.5 8.8 %copy-start.8 = (f32[4,320]{1,0:T(4,128)S(1)}, f32[4,320]{1,0:T(4,128)}, u32[]{:S(2)}) copy-start(f32[4,320]{1,0:T(4,128)} %param.29) | copy-start | bytes 15364
  10.5 8.9 %copy-start.9 = (f32[4,256]{1,0:T(4,128)S(1)}, f32[4,256]{1,0:T(4,128)}, u32[]{:S(2)}) copy-start(f32[4,256]{1,0:T(4,128)} %param.30) | copy-start | bytes 12292
  10.5 125.6 %all-to-all-start = ((bf16[16,64,2560]{2,1,0:T(8,128)(2,1)}), bf16[16,64,2560]{2,1,0:T(8,128)(2,1)}, u32[]{:S(2)}, u32[]{:S(2)}) async-start(bf16[16,64,2560]{2,1,0:T(8,128)(2,1)} %stack.2), calls=%async_computation | async-start | bytes 10485760 | tf_op jit(solution)/shard_map/all_to_all | solution.py:15
  19.2 208.1 %all-gather.7.cloned.1.call-start = ((), (), s32[]{:S(2)}) async-start(), calls=%async_computation.6 | async-start | bytes 1392640 | tf_op jit(solution)/shard_map/all_gather | solution.py:27
  19.4 120.3 %copy-start.6 = (f32[2560]{0:T(1024)S(1)}, f32[2560]{0:T(1024)}, u32[]{:S(2)}) copy-start(f32[2560]{0:T(1024)} %param.22) | copy-start | bytes 30724
  152.4 8.5 %slice-start = ((s8[5242880]{0:T(1024)(128)(4,1)}), s8[1048576]{0:T(1024)(128)(4,1)S(1)}, s32[]{:S(2)}) async-start(s8[5242880]{0:T(1024)(128)(4,1)} %bitcast.90), calls=%async_computation.7 | async-start | bytes 2097152
  152.8 8.1 %slice-start.1 = ((s8[5242880]{0:T(1024)(128)(4,1)}), s8[4194304]{0:T(1024)(128)(4,1)S(1)}, s32[]{:S(2)}) async-start(s8[5242880]{0:T(1024)(128)(4,1)} %bitcast.90), calls=%async_computation.8 | async-start | bytes 8388608
  152.8 8.1 %copy-start.12 = (bf16[2560,320]{0,1:T(8,128)(2,1)S(1)}, bf16[2560,320]{0,1:T(8,128)(2,1)}, u32[]{:S(2)}) copy-start(bf16[2560,320]{0,1:T(8,128)(2,1)} %param.24) | copy-start | bytes 4915204
  157.4 9.1 %collective-permute-start.1 = (bf16[3,256]{1,0:T(4,128)(2,1)S(1)}, bf16[3,256]{1,0:T(4,128)(2,1)S(1)}, u32[]{:S(2)}, u32[]{:S(2)}) collective-permute-start(bf16[3,256]{1,0:T(4,128)(2,1)S(1)} %slice.97), channel_id=1, source_target_pairs={{0,16},{16,32},{32,48},{48,64},{64,80},{80,96},{96,112},{112,128},... | collective-permute-start | bytes 4616 | tf_op jit(solution)/shard_map/ppermute | solution.py:21
  162.9 8.4 %collective-permute-start = (bf16[3,320]{0,1:T(8,128)(2,1)S(1)}, bf16[3,320]{0,1:T(8,128)(2,1)S(1)}, u32[]{:S(2)}, u32[]{:S(2)}) collective-permute-start(bf16[3,320]{0,1:T(8,128)(2,1)S(1)} %slice.92), channel_id=1, source_target_pairs={{0,16},{16,32},{32,48},{48,64},{64,80},{80,96},{96,112},{112,128},... | collective-permute-start | bytes 5768 | tf_op jit(solution)/shard_map/ppermute | solution.py:21
  179.1 4.0 copy-start.16
  183.0 163.8 %reduce-scatter.3.cloned.1.call-start = ((), (), s32[]{:S(2)}) async-start(), calls=%async_computation.3 | async-start | bytes 5570560 | tf_op jit(solution)/shard_map/reduce_scatter | solution.py:146
  224.9 10.8 %copy-start.11 = (f32[5]{0:T(128)S(1)}, f32[5]{0:T(128)}, u32[]{:S(2)}) copy-start(f32[5]{0:T(128)} %param.31) | copy-start | bytes 64
  227.3 12.5 %slice-start.2 = ((s8[5242880]{0:T(1024)(128)(4,1)}), s8[1048576]{0:T(1024)(128)(4,1)S(1)}, s32[]{:S(2)}) async-start(s8[5242880]{0:T(1024)(128)(4,1)} %bitcast.92), calls=%async_computation.9 | async-start | bytes 2097152
  235.6 4.2 slice-start.3
  239.8 4.7 copy-start.4
  241.4 27.1 %copy-start.14 = (f32[320]{0:T(512)S(1)}, f32[320]{0:T(512)}, u32[]{:S(2)}) copy-start(f32[320]{0:T(512)} %param.32) | copy-start | bytes 3844
  275.3 71.4 %copy-start.2 = (bf16[64,2560]{1,0:T(8,128)(2,1)S(1)}, bf16[64,2560]{1,0:T(8,128)(2,1)}, u32[]{:S(2)}) copy-start(bf16[64,2560]{1,0:T(8,128)(2,1)} %param.21) | copy-start | bytes 983044
  275.3 72.6 %copy-start.7 = (f32[2560]{0:T(1024)S(1)}, f32[2560]{0:T(1024)}, u32[]{:S(2)}) copy-start(f32[2560]{0:T(1024)} %param.34) | copy-start | bytes 30724
  275.3 116.3 %all-gather.5.cloned.1.call-start = ((), (), s32[]{:S(2)}) async-start(), calls=%async_computation.4 | async-start | bytes 5570560 | tf_op jit(solution)/shard_map/all_gather | solution.py:154
  349.8 121.2 %reduce-scatter.5.cloned.1.call-start = ((), (), s32[]{:S(2)}) async-start(), calls=%async_computation.5 | async-start | bytes 5570560 | tf_op jit(solution)/shard_map/reduce_scatter | solution.py:159
  407.0 64.0 %copy-start.3 = (bf16[64,2560]{1,0:T(8,128)(2,1)S(1)}, bf16[64,2560]{1,0:T(8,128)(2,1)}, u32[]{:S(2)}) copy-start(bf16[64,2560]{1,0:T(8,128)(2,1)} %reduce-scatter.3.cloned.1.call-done) | copy-start | bytes 983044
  (4 other events, 11.7 us)
Sparse Core Ops, SparseCore 0:
  183.1 44.1 all-gather.6
  275.5 71.2 reduce-scatter.2
  349.9 41.7 all-gather.4
  407.1 63.8 reduce-scatter.4
